TPU v7x, 512 devices: a whole 4x8x8 slice. The times are simulated.
512 devices in a mesh: replica: 32 (over x, y_hi, core), fsdp: 16 (over y_lo, z).
Axes of the slice: x: 4, y: 8 (y_hi: 4, y_lo: 2; y = y_hi * 2 + y_lo), z: 8, core: 2. Of those that a mesh axis runs over, the one named last changes fastest.
Arguments:
- numerators: float32 [32, 4096, 512], P('replica', 'fsdp'), may hold values from -6 to 6
- push_weights: float32 [32], P('replica'), may hold values from 0.5 to 2
- step_power: int32 [1], replicated, may hold values from 0 to 2
- activations: bfloat16 [32, 6144, 4096], P('replica', 'fsdp'), may hold values from -6 to 6
- targets: bfloat16 [32, 6144, 512], P('replica', 'fsdp'), may hold values from -6 to 6
- gain: float32 [4096], replicated, may hold values from 0.1 to 1.9
Outputs:
- mixed_numerators: float32 [32, 4096, 512], P('replica', 'fsdp')
- mixed_weights: float32 [32], P('replica')
All inputs are finite; a program needn't handle non-finite values.
Results may differ from a plain program's by a relative error of at most 0.015.
Values may be sent and summed in bfloat16 or wider, within the bound.
No kernel may reach another device: no remote copies, remote signals or barrier semaphores. Data moves between devices by JAX's collectives and lax.ppermute only.
A program may use at most 64 MiB of HBM per device.

v0:
```python
from functools import partial
import math
import jax
import jax.numpy as jnp
from jax import lax
from jax.sharding import PartitionSpec as P

DIST_KINDS = 3


def passed_along(value, axis, steps):
    count = lax.axis_size(axis)
    pairs = [(source, (source + steps) % count) for source in range(count)]
    return lax.ppermute(value, axis, pairs)


def send_updated(pair, by):
    return passed_along(pair, "replica", by)


def to_peer(sender, operand, power):
    branches = [partial(sender, by=1 << bit) for bit in range(DIST_KINDS)]
    return lax.switch(power, branches, operand)


def body(numerators, push_weights, step_power, activations, targets, gain):
    numer = numerators[0]
    power = step_power[0]
    features = activations.shape[2]
    replica_tokens = activations.shape[1] * lax.axis_size("fsdp")
    params = (numer / push_weights[0]).astype(jnp.bfloat16)
    act32 = activations[0].astype(jnp.float32)
    mean_sq = jnp.mean(act32 * act32, axis=1, keepdims=True)
    normed = (act32 * lax.rsqrt(mean_sq + 1e-05) * gain[None, :]).astype(jnp.bfloat16)
    columns = normed
    keys = jnp.dot(
        columns,
        lax.all_gather(params, "fsdp", axis=0, tiled=True),
        preferred_element_type=jnp.float32,
    ) / math.sqrt(features)
    errors = ((keys - targets[0].astype(jnp.float32)) / math.sqrt(replica_tokens)).astype(
        jnp.bfloat16
    )
    columns = normed
    grad = lax.psum_scatter(
        lax.dot_general(
            columns, errors, (((0,), (0,)), ((), ())), preferred_element_type=jnp.float32
        ).astype(jnp.bfloat16),
        "fsdp",
        scatter_dimension=0,
        tiled=True,
    ).astype(jnp.float32)
    updated = numer - 0.3 * grad
    peer_updated, peer_weight = to_peer(send_updated, (updated, push_weights), power)
    mixed_numerators = 0.5 * (updated + peer_updated)
    mixed_weights = 0.5 * (push_weights + peer_weight)
    return (mixed_numerators[None], mixed_weights)


def solution(mesh):
    return jax.shard_map(
        body,
        mesh=mesh,
        in_specs=(
            P("replica", "fsdp", None),
            P("replica"),
            P(),
            P("replica", "fsdp", None),
            P("replica", "fsdp", None),
            P(),
        ),
        out_specs=(P("replica", "fsdp", None), P("replica")),
        check_vma=False,
    )
```

profile of v0, /device:TPU:8, one launch (start us, length us, event | category | flops | bytes accessed | tf_op | source)
XLA Modules:
  0.0 219.8 jit_solution(8398441809625169285)
XLA Ops:
  7.2 0.0 copy-start
  7.2 0.0 copy-start.2
  7.2 0.0 all-gather.2.cloned.1.call-start
  8.0 2.0 fusion.8
  10.0 0.0 all-gather.2.cloned.1.call-update
  10.1 0.0 reduce-scatter.2.cloned.1.call-start
  10.1 2.6 %fusion = f32[384]{0:T(512)S(1)} fusion(bf16[1,384,4096]{2,1,0:T(8,128)(2,1)} %param.12), kind=kLoop, calls=%fused_computation.2 | loop fusion | flops 4718208 | bytes 3147264 | tf_op jit(solution)/shard_map/reduce_sum | solution.py:33
  12.7 80.8 %all-gather.2.cloned.1.call-done = bf16[4096,512]{1,0:T(8,128)(2,1)} async-done(((bf16[256,512]{1,0:T(8,128)(2,1)}), bf16[4096,512]{1,0:T(8,128)(2,1)}) %all-gather.2.cloned.1.call-update) | async-done | bytes 4194320 | tf_op jit(solution)/shard_map/all_gather | solution.py:38
  93.5 0.0 copy-done
  93.5 0.0 copy-done.2
  93.5 8.4 %convolution_convert_fusion = bf16[4096,512]{1,0:T(8,128)(2,1)} fusion(bf16[1,384,4096]{2,1,0:T(8,128)(2,1)S(1)} %copy-done, f32[4096]{0:T(1024)} %param.14, f32[384]{0:T(512)S(1)} %add_rsqrt_fusion, bf16[4096,512]{1,0:T(8,128)(2,1)} %all-gather.2.cloned.1.call-done, bf16[1,384,512]{2,1,0:T(8,128)(2,1)S(1)} %copy-done.2), kind=kOutput, calls=%fused_computation.5 | convolution fusion | flops 3236888576 | bytes 11945472 | tf_op jit(solution)/shard_map/dot_general | solution.py:46
  101.9 0.0 copy-start.1
  101.9 0.0 reduce-scatter.2.cloned.1.call-update
  102.6 81.1 %reduce-scatter.2.cloned.1.call-done = bf16[256,512]{1,0:T(8,128)(2,1)} async-done(((bf16[4096,512]{1,0:T(8,128)(2,1)}), bf16[256,512]{1,0:T(8,128)(2,1)}) %reduce-scatter.2.cloned.1.call-update) | async-done | bytes 262160 | tf_op jit(solution)/shard_map/reduce_scatter | solution.py:45
  183.7 0.0 copy-done.1
  183.7 1.0 bitcast_subtract_fusion
  184.8 24.5 %conditional.1 = (f32[256,512]{1,0:T(8,128)}, f32[1]{0:T(128)}) conditional(s32[]{:T(128)} %bitcast.5, (f32[256,512]{1,0:T(8,128)S(1)}, f32[1]{0:T(128)}) %tuple.20, (f32[256,512]{1,0:T(8,128)S(1)}, f32[1]{0:T(128)}) %tuple.20, (f32[256,512]{1,0:T(8,128)S(1)}, f32[1]{0:T(128)}) %tuple.20), branch_computations={%region_2.0_spmd, %region_3.0_spmd, %region_4.0_spmd} | conditional | bytes 2097264 | solution.py:23
  184.8 8.9 %collective-permute-start.4 = (f32[256,512]{1,0:T(8,128)S(1)}, f32[256,512]{1,0:T(8,128)}, u32[]{:S(2)}, u32[]{:S(2)}) collective-permute-start(f32[256,512]{1,0:T(8,128)S(1)} %get-tuple-element.16), channel_id=1, source_target_pairs={{0,64},{16,80},{32,96},{48,112},{64,128},{80,144},{96,160},{112,17... | collective-permute-start | bytes 1572872 | tf_op jit(solution)/shard_map/cond/branch_2_fun/ppermute | solution.py:14
  193.7 1.9 collective-permute-start.5
  195.6 13.6 %collective-permute-done.5 = f32[1]{0:T(128)} collective-permute-done((f32[1]{0:T(128)}, f32[1]{0:T(128)}, u32[]{:S(2)}, u32[]{:S(2)}) %collective-permute-start.5) | collective-permute-done | bytes 36 | tf_op jit(solution)/shard_map/cond/branch_2_fun/ppermute | solution.py:14
  209.2 0.0 collective-permute-done.4
  209.2 1.9 multiply_bitcast_fusion
  (1 shorter events, 0.0 us)
Async XLA Ops:
  7.2 86.4 %copy-start = (bf16[1,384,4096]{2,1,0:T(8,128)(2,1)S(1)}, bf16[1,384,4096]{2,1,0:T(8,128)(2,1)}, u32[]{:S(2)}) copy-start(bf16[1,384,4096]{2,1,0:T(8,128)(2,1)} %param.12) | copy-start | bytes 9437188
  7.2 86.3 %copy-start.2 = (bf16[1,384,512]{2,1,0:T(8,128)(2,1)S(1)}, bf16[1,384,512]{2,1,0:T(8,128)(2,1)}, u32[]{:S(2)}) copy-start(bf16[1,384,512]{2,1,0:T(8,128)(2,1)} %param.13) | copy-start | bytes 1179652
  7.2 86.3 %all-gather.2.cloned.1.call-start = ((), (), s32[]{:S(2)}) async-start(), calls=%async_computation.1 | async-start | bytes 4456448 | tf_op jit(solution)/shard_map/all_gather | solution.py:38
  10.1 173.7 %reduce-scatter.2.cloned.1.call-start = ((), (), s32[]{:S(2)}) async-start(), calls=%async_computation.2 | async-start | bytes 4456448 | tf_op jit(solution)/shard_map/reduce_scatter | solution.py:45
  101.9 81.9 %copy-start.1 = (f32[1,256,512]{2,1,0:T(8,128)S(1)}, f32[1,256,512]{2,1,0:T(8,128)}, u32[]{:S(2)}) copy-start(f32[1,256,512]{2,1,0:T(8,128)} %param.9) | copy-start | bytes 1572868
  184.8 24.4 %collective-permute-start.4 = (f32[256,512]{1,0:T(8,128)S(1)}, f32[256,512]{1,0:T(8,128)}, u32[]{:S(2)}, u32[]{:S(2)}) collective-permute-start(f32[256,512]{1,0:T(8,128)S(1)} %get-tuple-element.16), channel_id=1, source_target_pairs={{0,64},{16,80},{32,96},{48,112},{64,128},{80,144},{96,160},{112,17... | collective-permute-start | bytes 1572872 | tf_op jit(solution)/shard_map/cond/branch_2_fun/ppermute | solution.py:14
  193.7 15.5 %collective-permute-start.5 = (f32[1]{0:T(128)}, f32[1]{0:T(128)}, u32[]{:S(2)}, u32[]{:S(2)}) collective-permute-start(f32[1]{0:T(128)} %get-tuple-element.17), channel_id=1, source_target_pairs={{0,64},{16,80},{32,96},{48,112},{64,128},{80,144},{96,160},{112,17... | collective-permute-start | bytes 20 | tf_op jit(solution)/shard_map/cond/branch_2_fun/ppermute | solution.py:14
Sparse Core Ops, SparseCore 0:
  10.6 82.8 all-gather.1
  102.0 81.6 reduce-scatter.1
where the time goes:
time: 220 us
  waiting for transfers between devices  176 us (80%)
  between operations  17.3 us (8%)
  starting transfers between devices  10.9 us (5%)
  matrix products  8.36 us (4%)
  other arithmetic  7.54 us (3%)
    reduce_scatter x1, waiting for transfers between devices, body(): lax.psum_scatter(lax.dot_general(columns, errors, (((0,), (0,)), ((), ())...  81.1 us
    all_gather x1, waiting for transfers between devices, body(): lax.all_gather(params, 'fsdp', axis=0, tiled=True)  80.8 us
    ppermute x2, waiting for transfers between devices, passed_along(): return lax.ppermute(value, axis, pairs)  13.6 us
    ppermute x2, starting transfers between devices, passed_along(): return lax.ppermute(value, axis, pairs)  10.8 us
    dot_general x1, matrix products, body(): lax.dot_general(columns, errors, (((0,), (0,)), ((), ())), preferred_elem...  8.36 us
  transfers between devices with their start and end apart: 4, of which 3 were waited for; matrix products, arithmetic and copies ran while one was open for 1% of the time, Pallas kernels for 0%

commit v1 on v0

--- a/solution.py
+++ b/solution.py
@@ -1,3 +1,4 @@
+import functools
 from functools import partial
 import math
 import jax
@@ -6,6 +7,15 @@
 from jax.sharding import PartitionSpec as P
 
 DIST_KINDS = 3
+
+
+def assign_local_data(page, axis_name, at_axis):
+    frame_out = jnp.stack(lax.axis_size(axis_name) * [page])
+    step_out = lax.all_to_all(frame_out, axis_name, split_axis=0, concat_axis=0)
+    return jnp.concatenate(step_out, axis=at_axis)
+
+
+drive_loops = functools.partial(assign_local_data, axis_name="fsdp", at_axis=0)
 
 
 def passed_along(value, axis, steps):
@@ -33,11 +43,9 @@
     mean_sq = jnp.mean(act32 * act32, axis=1, keepdims=True)
     normed = (act32 * lax.rsqrt(mean_sq + 1e-05) * gain[None, :]).astype(jnp.bfloat16)
     columns = normed
-    keys = jnp.dot(
-        columns,
-        lax.all_gather(params, "fsdp", axis=0, tiled=True),
-        preferred_element_type=jnp.float32,
-    ) / math.sqrt(features)
+    keys = jnp.dot(columns, drive_loops(params), preferred_element_type=jnp.float32) / math.sqrt(
+        features
+    )
     errors = ((keys - targets[0].astype(jnp.float32)) / math.sqrt(replica_tokens)).astype(
         jnp.bfloat16
     )

time: 220 us -> 258 us (1.17)
  the two profiles are of different devices: /device:TPU:8 before, /device:TPU:24 now
where the time goes in v1:
time: 258 us; the launch traced here: 257 us
  waiting for transfers between devices  201 us (78%)
  starting transfers between devices  24 us (9%)
  between operations  17.1 us (7%)
  matrix products  8.38 us (3%)
  other arithmetic  4.73 us (2%)
    all_to_all x1, waiting for transfers between devices, assign_local_data(): step_out = lax.all_to_all(frame_out, axis_name, split_axis=0, concat_axis=0)  105 us
    reduce_scatter x1, waiting for transfers between devices, body(): lax.psum_scatter(lax.dot_general(columns, errors, (((0,), (0,)), ((), ())...  82.4 us
    ppermute x2, waiting for transfers between devices, passed_along(): return lax.ppermute(value, axis, pairs)  12.8 us
    all_to_all x1, starting transfers between devices, assign_local_data(): step_out = lax.all_to_all(frame_out, axis_name, split_axis=0, concat_axis=0)  12.1 us
    ppermute x2, starting transfers between devices, passed_along(): return lax.ppermute(value, axis, pairs)  12 us
    dot_general x1, matrix products, body(): lax.dot_general(columns, errors, (((0,), (0,)), ((), ())), preferred_elem...  8.38 us
  transfers between devices with their start and end apart: 4, of which 3 were waited for; matrix products, arithmetic and copies ran while one was open for 0% of the time, Pallas kernels for 0%

profile of v1, /device:TPU:24, one launch (start us, length us, event | category | flops | bytes accessed | tf_op | source)
XLA Modules:
  0.0 257.3 jit_solution(362780594197579538)
XLA Ops:
  7.8 1.1 fusion.27
  8.9 2.4 stack.5
  11.3 0.0 copy-start
  11.3 0.0 copy-start.2
  11.3 12.1 %all-to-all-start = ((bf16[16,256,512]{2,1,0:T(8,128)(2,1)}), bf16[16,256,512]{2,1,0:T(8,128)(2,1)}, u32[]{:S(2)}, u32[]{:S(2)}) async-start(bf16[16,256,512]{2,1,0:T(8,128)(2,1)} %stack.5), calls=%async_computation | async-start | bytes 8388608 | tf_op jit(solution)/shard_map/all_to_all | solution.py:14
  23.3 0.0 reduce-scatter.2.cloned.1.call-start
  23.4 0.0 copy-done
  23.4 0.7 fusion.2
  24.1 105.3 %all-to-all-done = bf16[16,256,512]{2,1,0:T(8,128)(2,1)} async-done(((bf16[16,256,512]{2,1,0:T(8,128)(2,1)}), bf16[16,256,512]{2,1,0:T(8,128)(2,1)}, u32[]{:S(2)}, u32[]{:S(2)}) %all-to-all-start) | async-done | bytes 4194336 | tf_op jit(solution)/shard_map/all_to_all | solution.py:14
  129.4 0.0 copy-done.2
  129.4 8.4 %convolution_convert_fusion = bf16[4096,512]{1,0:T(8,128)(2,1)} fusion(bf16[1,384,4096]{2,1,0:T(8,128)(2,1)S(1)} %copy-done, f32[4096]{0:T(1024)} %param.14, f32[384]{0:T(512)S(1)} %add_rsqrt_fusion, bf16[4096,512]{1,0:T(8,128)(2,1)} %bitcast.5, bf16[1,384,512]{2,1,0:T(8,128)(2,1)S(1)} %copy-done.2), kind=kOutput, calls=%fused_computation.9 | convolution fusion | flops 3236888576 | bytes 11945472 | tf_op jit(solution)/shard_map/dot_general | solution.py:54
  137.8 0.0 copy-start.1
  137.8 0.0 reduce-scatter.2.cloned.1.call-update
  138.5 82.4 %reduce-scatter.2.cloned.1.call-done = bf16[256,512]{1,0:T(8,128)(2,1)} async-done(((bf16[4096,512]{1,0:T(8,128)(2,1)}), bf16[256,512]{1,0:T(8,128)(2,1)}) %reduce-scatter.2.cloned.1.call-update) | async-done | bytes 262160 | tf_op jit(solution)/shard_map/reduce_scatter | solution.py:53
  220.9 0.0 copy-done.1
  220.9 1.0 bitcast_subtract_fusion
  222.0 24.8 %conditional.1 = (f32[256,512]{1,0:T(8,128)}, f32[1]{0:T(128)}) conditional(s32[]{:T(128)} %bitcast.7, (f32[256,512]{1,0:T(8,128)S(1)}, f32[1]{0:T(128)}) %tuple.20, (f32[256,512]{1,0:T(8,128)S(1)}, f32[1]{0:T(128)}) %tuple.20, (f32[256,512]{1,0:T(8,128)S(1)}, f32[1]{0:T(128)}) %tuple.20), branch_computations={%region_2.0_spmd, %region_3.0_spmd, %region_4.0_spmd} | conditional | bytes 2097264 | solution.py:33
  222.0 10.0 %collective-permute-start.4 = (f32[256,512]{1,0:T(8,128)S(1)}, f32[256,512]{1,0:T(8,128)}, u32[]{:S(2)}, u32[]{:S(2)}) collective-permute-start(f32[256,512]{1,0:T(8,128)S(1)} %get-tuple-element.16), channel_id=1, source_target_pairs={{0,64},{16,80},{32,96},{48,112},{64,128},{80,144},{96,160},{112,17... | collective-permute-start | bytes 1572872 | tf_op jit(solution)/shard_map/cond/branch_2_fun/ppermute | solution.py:24
  232.0 1.9 collective-permute-start.5
  233.9 12.8 %collective-permute-done.5 = f32[1]{0:T(128)} collective-permute-done((f32[1]{0:T(128)}, f32[1]{0:T(128)}, u32[]{:S(2)}, u32[]{:S(2)}) %collective-permute-start.5) | collective-permute-done | bytes 36 | tf_op jit(solution)/shard_map/cond/branch_2_fun/ppermute | solution.py:24
  246.8 0.0 collective-permute-done.4
  246.8 1.9 multiply_bitcast_fusion
  (1 shorter events, 0.0 us)
Async XLA Ops:
  11.3 12.1 %copy-start = (bf16[1,384,4096]{2,1,0:T(8,128)(2,1)S(1)}, bf16[1,384,4096]{2,1,0:T(8,128)(2,1)}, u32[]{:S(2)}) copy-start(bf16[1,384,4096]{2,1,0:T(8,128)(2,1)} %param.12) | copy-start | bytes 9437188
  11.3 118.1 %copy-start.2 = (bf16[1,384,512]{2,1,0:T(8,128)(2,1)S(1)}, bf16[1,384,512]{2,1,0:T(8,128)(2,1)}, u32[]{:S(2)}) copy-start(bf16[1,384,512]{2,1,0:T(8,128)(2,1)} %param.13) | copy-start | bytes 1179652
  11.3 118.1 %all-to-all-start = ((bf16[16,256,512]{2,1,0:T(8,128)(2,1)}), bf16[16,256,512]{2,1,0:T(8,128)(2,1)}, u32[]{:S(2)}, u32[]{:S(2)}) async-start(bf16[16,256,512]{2,1,0:T(8,128)(2,1)} %stack.5), calls=%async_computation | async-start | bytes 8388608 | tf_op jit(solution)/shard_map/all_to_all | solution.py:14
  23.3 197.6 %reduce-scatter.2.cloned.1.call-start = ((), (), s32[]{:S(2)}) async-start(), calls=%async_computation.2 | async-start | bytes 4456448 | tf_op jit(solution)/shard_map/reduce_scatter | solution.py:53
  137.8 83.1 %copy-start.1 = (f32[1,256,512]{2,1,0:T(8,128)S(1)}, f32[1,256,512]{2,1,0:T(8,128)}, u32[]{:S(2)}) copy-start(f32[1,256,512]{2,1,0:T(8,128)} %param.9) | copy-start | bytes 1572868
  222.0 24.8 %collective-permute-start.4 = (f32[256,512]{1,0:T(8,128)S(1)}, f32[256,512]{1,0:T(8,128)}, u32[]{:S(2)}, u32[]{:S(2)}) collective-permute-start(f32[256,512]{1,0:T(8,128)S(1)} %get-tuple-element.16), channel_id=1, source_target_pairs={{0,64},{16,80},{32,96},{48,112},{64,128},{80,144},{96,160},{112,17... | collective-permute-start | bytes 1572872 | tf_op jit(solution)/shard_map/cond/branch_2_fun/ppermute | solution.py:24
  232.0 14.8 %collective-permute-start.5 = (f32[1]{0:T(128)}, f32[1]{0:T(128)}, u32[]{:S(2)}, u32[]{:S(2)}) collective-permute-start(f32[1]{0:T(128)} %get-tuple-element.17), channel_id=1, source_target_pairs={{0,64},{16,80},{32,96},{48,112},{64,128},{80,144},{96,160},{112,17... | collective-permute-start | bytes 20 | tf_op jit(solution)/shard_map/cond/branch_2_fun/ppermute | solution.py:24
Sparse Core Ops, SparseCore 0:
  137.9 82.9 reduce-scatter.1
